TPU v7x, 128 devices: a whole 4x4x4 slice. The times are simulated.
128 devices in a mesh: dp: 32 (over y, x, core), mp: 4 (over z).
Axes of the slice: x: 4, y: 4, z: 4, core: 2. Of those that a mesh axis runs over, the one named last changes fastest.
Arguments:
- hidden: bfloat16 [4096, 2560], P('dp', 'mp'), may hold values from -6 to 6
- norm_gain: bfloat16 [2560], replicated, may hold values from 0.5 to 1.5
- shared_gate: bfloat16 [2560, 3072], P(None, 'mp'), may hold values from -0.125 to 0.125
- shared_up: bfloat16 [2560, 3072], P(None, 'mp'), may hold values from -0.125 to 0.125
- shared_down: bfloat16 [3072, 2560], P('mp'), may hold values from -0.109375 to 0.109375
- expert_gate: bfloat16 [64, 2560, 1536], P('dp', None, 'mp'), may hold values from -0.125 to 0.125
- expert_up: bfloat16 [64, 2560, 1536], P('dp', None, 'mp'), may hold values from -0.125 to 0.125
- expert_down: bfloat16 [64, 1536, 2560], P('dp', 'mp'), may hold values from -0.15625 to 0.15625
- adapter_in: bfloat16 [64, 3072, 16], P('dp', 'mp'), may hold values from -0.109375 to 0.109375
- adapter_out: bfloat16 [64, 16, 2560], P('dp'), may hold values from -1.5 to 1.5
- active: int32 [16], replicated, may hold values from 0 to 63, as said below
- lengths: int32 [64], replicated, may hold values from 1 to 1024, 4096 in all
- request_adapter: int32 [64], replicated, may hold values from 0 to 15
- routes: int32 [4096, 6], P('dp'), may hold values from 0 to 63, all different within a row; in each aligned block of 128 rows (0 to 127, 128 to 255, ...) at most 16 rows name the same one
- route_weights: float32 [4096, 6], P('dp'), may hold values from 0.05 to 0.35
Outputs:
- layer_out: bfloat16 [4096, 2560], P('dp', 'mp')
Inputs may be any that keep to these rules, and one draw needn't show every extreme that they name: `active`: the entries are distinct. `routes`: within the 128 rows of one index of dp no expert is named more than 16 times, and that many is reached; a row names distinct experts.
All inputs are finite; a program needn't handle non-finite values.
Results may differ from a plain program's by a relative error of at most 0.015.
Values may be sent and summed in bfloat16 or wider, within the bound.
No kernel may reach another device: no remote copies, remote signals or barrier semaphores. Data moves between devices by JAX's collectives and lax.ppermute only.
A program may use at most 128 MiB of HBM per device.

v0:
```python
import jax
import jax.numpy as jnp
from jax import lax
from jax.sharding import PartitionSpec as P


def experts_apply(slots_in, expert_gate, expert_up, expert_down):
    gate_val = jnp.einsum(
        "sjcd,jdf->sjcf", slots_in, expert_gate, preferred_element_type=jnp.float32
    )
    up_val = jnp.einsum("sjcd,jdf->sjcf", slots_in, expert_up, preferred_element_type=jnp.float32)
    inner = (jax.nn.silu(gate_val) * up_val).astype(jnp.bfloat16)
    return jnp.einsum("sjcf,jfd->sjcd", inner, expert_down, preferred_element_type=jnp.float32)


def body(
    hidden,
    norm_gain,
    shared_gate,
    shared_up,
    shared_down,
    expert_gate,
    expert_up,
    expert_down,
    adapter_in,
    adapter_out,
    active,
    lengths,
    request_adapter,
    routes,
    route_weights,
):
    tok_rows = routes.shape[0]
    top_count = routes.shape[1]
    dp_count = lax.axis_size("dp")
    mp_count = lax.axis_size("mp")
    dp_index = lax.axis_index("dp")
    mp_index = lax.axis_index("mp")
    local_experts = expert_gate.shape[0]
    total_experts = local_experts * dp_count
    capacity = mp_count * max(1, tok_rows * top_count * 4 // (total_experts * mp_count * 3))
    col_width = hidden.shape[1]
    col_start = mp_index * col_width
    active_count = active.shape[0]
    rank_width = adapter_in.shape[2]
    local_adapters = adapter_in.shape[0]
    owned_ids = dp_index * local_adapters + jnp.arange(local_adapters, dtype=jnp.int32)
    selector = (active[:, None] == owned_ids[None, :]).astype(jnp.bfloat16)
    out_cols = lax.dynamic_slice_in_dim(adapter_out, col_start, col_width, axis=2)
    picked_in = jnp.einsum(
        "ji,isr->jsr", selector, adapter_in, preferred_element_type=jnp.float32
    ).astype(jnp.bfloat16)
    picked_out = jnp.einsum(
        "ji,ird->jrd", selector, out_cols, preferred_element_type=jnp.float32
    ).astype(jnp.bfloat16)
    picked_in, picked_out = lax.psum((picked_in, picked_out), "dp")
    gathered = lax.all_gather(hidden, "mp", axis=1, tiled=True)
    values = gathered.astype(jnp.float32)
    factor = lax.rsqrt(jnp.mean(values * values, axis=-1, keepdims=True) + 1e-06)
    normed = (values * factor * norm_gain.astype(jnp.float32)).astype(jnp.bfloat16)
    width = normed.shape[1]
    shared_lin = jnp.dot(normed, shared_gate, preferred_element_type=jnp.float32)
    shared_pre = jnp.dot(normed, shared_up, preferred_element_type=jnp.float32)
    shared_act = (jax.nn.silu(shared_lin) * shared_pre).astype(jnp.bfloat16)
    request_end = jnp.cumsum(lengths)
    positions = dp_index * tok_rows + jnp.arange(tok_rows, dtype=jnp.int32)
    request_of = jnp.sum((request_end[None, :] <= positions[:, None]).astype(jnp.int32), axis=1)
    request_hot = (
        request_of[:, None] == jnp.arange(lengths.shape[0], dtype=jnp.int32)[None, :]
    ).astype(jnp.int32)
    slot_of = jnp.sum(request_hot * request_adapter[None, :], axis=1)
    chosen = (slot_of[:, None] == jnp.arange(active_count, dtype=jnp.int32)[None, :]).astype(
        jnp.float32
    )
    in_matrix = jnp.transpose(picked_in, (1, 0, 2)).reshape(
        shared_act.shape[1], active_count * rank_width
    )
    lowrank = jnp.dot(shared_act, in_matrix, preferred_element_type=jnp.float32)
    lowrank_sel = jnp.sum(
        lowrank.reshape(tok_rows, active_count, rank_width) * chosen[:, :, None], axis=1
    )
    lowrank_sel = lax.psum(lowrank_sel, "mp")
    lowrank = (chosen[:, :, None] * lowrank_sel[:, None, :]).reshape(
        tok_rows, active_count * rank_width
    )
    adapted = jnp.dot(
        lowrank,
        picked_out.reshape(active_count * rank_width, col_width).astype(jnp.float32),
        precision=lax.Precision.HIGHEST,
    )
    flat_routes = routes.reshape(-1)
    expert_hot = (
        flat_routes[:, None] == jnp.arange(total_experts, dtype=jnp.int32)[None, :]
    ).astype(jnp.int32)
    earlier = jnp.cumsum(expert_hot, axis=0) - expert_hot
    position = jnp.sum(earlier * expert_hot, axis=1)
    slot_index = (flat_routes * capacity + position).reshape(tok_rows, top_count)
    slot_count = total_experts * capacity
    slot_hit = slot_index[:, :, None] == jnp.arange(slot_count, dtype=jnp.int32)[None, None, :]
    dispatch = jnp.any(slot_hit, axis=1).astype(jnp.bfloat16)
    send_rows = jnp.einsum(
        "ts,td->sd", dispatch, normed, preferred_element_type=jnp.float32
    ).astype(jnp.bfloat16)
    send_rows = send_rows.reshape(dp_count, local_experts, capacity, width)
    returned = lax.all_to_all(
        experts_apply(
            lax.all_to_all(send_rows, "dp", split_axis=0, concat_axis=0, tiled=True),
            expert_gate,
            expert_up,
            expert_down,
        ).astype(jnp.bfloat16),
        "dp",
        split_axis=0,
        concat_axis=0,
        tiled=True,
    )
    returned = returned.reshape(slot_count, width)
    combine = jnp.sum(jnp.where(slot_hit, route_weights[:, :, None], 0.0), axis=1)
    combine_hi = combine.astype(jnp.bfloat16)
    combine_lo = (combine - combine_hi.astype(jnp.float32)).astype(jnp.bfloat16)
    routed = jnp.dot(combine_hi, returned, preferred_element_type=jnp.float32) + jnp.dot(
        combine_lo, returned, preferred_element_type=jnp.float32
    )
    partial_out = jnp.dot(shared_act, shared_down, preferred_element_type=jnp.float32) + routed
    own_cols = lax.dynamic_slice_in_dim(partial_out, col_start, col_width, axis=1) + adapted
    partial_out = lax.dynamic_update_slice_in_dim(partial_out, own_cols, col_start, axis=1)
    return lax.psum_scatter(partial_out.astype(jnp.bfloat16), "mp", scatter_dimension=1, tiled=True)


def solution(mesh):
    in_specs = (
        P("dp", "mp"),
        P(),
        P(None, "mp"),
        P(None, "mp"),
        P("mp", None),
        P("dp", None, "mp"),
        P("dp", None, "mp"),
        P("dp", "mp", None),
        P("dp", "mp", None),
        P("dp", None, None),
        P(),
        P(),
        P(),
        P("dp", None),
        P("dp", None),
    )
    out_specs = P("dp", "mp")
    return jax.shard_map(body, mesh=mesh, in_specs=in_specs, out_specs=out_specs, check_vma=False)
```

profile of v0, /device:TPU:0, one launch (start us, length us, event | category | flops | bytes accessed | tf_op | source)
XLA Modules:
  0.0 315.9 jit_solution(4285871344129331172)
XLA Ops:
  6.5 0.8 copy.60
  7.7 1.8 reduce-window.18
  10.1 0.7 multiply_add_fusion
  11.3 14.9 %all_gather.3 = bf16[128,2560]{1,0:T(8,128)(2,1)S(1)} all-gather(bf16[128,640]{1,0:T(8,128)(2,1)} %param.15), channel_id=1, replica_groups=mesh['dp'=32,'mp'=4] {'mp'}, dimensions={1}, use_global_device_ids=true | all-gather | bytes 819200 | tf_op jit(solution)/shard_map/all_gather | solution.py:57
  27.2 1.6 convolution_convert_fusion.1
  28.8 69.5 %all_to_all.10 = bf16[32,2,16,2560]{3,2,1,0:T(8,128)(2,1)S(1)} all-to-all(bf16[32,2,16,2560]{3,2,1,0:T(8,128)(2,1)S(1)} %bitcast.98), channel_id=1, replica_groups=mesh['dp'=32,'mp'=4] {'dp'}, dimensions={0} | all-to-all | bytes 10485760 | tf_op jit(solution)/shard_map/all_to_all | solution.py:107
  98.3 2.3 copy-done.1
  100.6 2.9 fusion.3
  103.5 12.8 %fusion = bf16[32,2,16,2560]{3,2,0,1:T(8,128)(2,1)} fusion(bf16[2,384,2560]{2,1,0:T(8,128)(2,1)} %param.22, f32[2,32,16,384]{3,2,1,0:T(8,128)S(1)} %fusion.3, bf16[2,2560,384]{2,1,0:T(8,128)(2,1)} %param.21, bf16[32,2,16,2560]{3,2,1,0:T(8,128)(2,1)} %copy-done.1), kind=kOutput, calls=%fused_computation.2 | convolution fusion | flops 4031512576 | bytes 19922944 | tf_op jit(solution)/shard_map/sjcf,jfd->sjcd/dot_general | solution.py:13
  116.3 5.3 %copy.66 = bf16[32,2,16,2560]{3,2,1,0:T(8,128)(2,1)} copy(bf16[32,2,16,2560]{3,2,0,1:T(8,128)(2,1)} %fusion) | data formatting | bytes 10485760 | tf_op jit(solution)/shard_map/convert_element_type | solution.py:111
  121.5 5.0 %all-to-all-start.1 = ((bf16[32,2,16,2560]{3,2,1,0:T(8,128)(2,1)}), bf16[32,2,16,2560]{3,2,1,0:T(8,128)(2,1)}, u32[]{:S(2)}, u32[]{:S(2)}) async-start(bf16[32,2,16,2560]{3,2,1,0:T(8,128)(2,1)} %copy.66), calls=%async_computation.1 | async-start | bytes 10485760 | tf_op jit(solution)/shard_map/all_to_all | solution.py:105
  127.1 0.9 copy.95
  128.0 1.1 convolution_convert_fusion.3
  130.3 3.2 fusion.57
  133.5 0.8 fusion.26
  134.3 1.3 copy-done.2
  136.3 131.0 %all-reduce.3.cloned.1.call-done = (bf16[16,16,640]{2,0,1:T(8,128)(2,1)}, bf16[16,16,768]{2,1,0:T(8,128)(2,1)}) async-done(((bf16[16,16,640]{2,0,1:T(8,128)(2,1)}, bf16[16,16,768]{2,1,0:T(8,128)(2,1)}), (bf16[16,16,640]{2,0,1:T(8,128)(2,1)}, bf16[16,16,768]{2,1,0:T(8,128)(2,1)})) %all-reduce.3.cloned.1.call-update) | async-done | bytes 720912 | tf_op jit(solution)/shard_map/psum | solution.py:56
  267.3 1.3 fusion.29
  268.6 10.8 %psum.22 = f32[128,16]{0,1:T(8,128)S(1)} all-reduce(f32[128,16]{0,1:T(8,128)S(1)} %fusion.29), channel_id=1, replica_groups=mesh['dp'=32,'mp'=4] {'mp'}, use_global_device_ids=true, to_apply=%region_11.12 | all-reduce | flops 2048 | bytes 16384 | tf_op jit(solution)/shard_map/psum | solution.py:82
  279.4 3.3 %fusion.39 = f32[128,2560]{1,0:T(8,128)S(1)} fusion(bf16[1024,2560]{1,0:T(8,128)(2,1)} %bitcast.11, f32[128,1024]{1,0:T(8,128)S(1)} %select_reduce_fusion), kind=kOutput, calls=%fused_computation.53 | convolution fusion | flops 671219712 | bytes 7077888 | tf_op jit(solution)/shard_map/dot_general | solution.py:121
  282.7 3.5 %fusion.8 = f32[128,2560]{1,0:T(8,128)S(1)} fusion(f32[128,2560]{1,0:T(8,128)S(1)} %fusion.59, f32[128,2560]{1,0:T(8,128)S(1)} %fusion.39, bf16[1024,2560]{1,0:T(8,128)(2,1)} %bitcast.11, f32[128,1024]{1,0:T(8,128)S(1)} %select_reduce_fusion), kind=kOutput, calls=%fused_computation.11 | convolution fusion | flops 672268288 | bytes 9699328 | tf_op jit(solution)/shard_map/dot_general | solution.py:121
  286.7 1.1 copy.75
  287.8 19.6 %reduce-scatter.4.cloned.1.call-done = bf16[640,128]{1,0:T(8,128)(2,1)} async-done(((bf16[2560,128]{1,0:T(8,128)(2,1)}), bf16[640,128]{1,0:T(8,128)(2,1)}) %reduce-scatter.4.cloned.1.call-update) | async-done | bytes 163856
  307.4 1.7 copy.76
  (51 shorter events, 5.1 us)
Async XLA Ops:
  6.5 121.4 %copy-start = (bf16[2,16,2560]{2,1,0:T(8,128)(2,1)S(1)}, bf16[2,16,2560]{2,1,0:T(8,128)(2,1)}, u32[]{:S(2)}) copy-start(bf16[2,16,2560]{2,1,0:T(8,128)(2,1)} %param.24) | copy-start | bytes 491524
  28.8 71.8 %copy-start.8 = (bf16[2,2560,384]{2,1,0:T(8,128)(2,1)S(1)}, bf16[2,2560,384]{2,1,0:T(8,128)(2,1)}, u32[]{:S(2)}) copy-start(bf16[2,2560,384]{2,1,0:T(8,128)(2,1)} %param.20) | copy-start | bytes 11796484
  98.3 2.3 copy-start.1
  121.5 5.1 %copy-start.4 = (bf16[2,768,16]{1,2,0:T(8,128)(2,1)S(1)}, bf16[2,768,16]{1,2,0:T(8,128)(2,1)}, u32[]{:S(2)}) copy-start(bf16[2,768,16]{1,2,0:T(8,128)(2,1)} %param.23) | copy-start | bytes 147460
  121.5 5.1 %copy-start.6 = (s32[16]{0:T(128)S(1)}, s32[16]{0:T(128)}, u32[]{:S(2)}) copy-start(s32[16]{0:T(128)} %param.25) | copy-start | bytes 196
  121.5 7.8 %copy-start.7 = (s32[64]{0:T(128)S(1)}, s32[64]{0:T(128)}, u32[]{:S(2)}) copy-start(s32[64]{0:T(128)} %param.26) | copy-start | bytes 772
  121.5 8.2 %copy-start.10 = (s32[64]{0:T(128)S(1)}, s32[64]{0:T(128)}, u32[]{:S(2)}) copy-start(s32[64]{0:T(128)} %param.27) | copy-start | bytes 772
  121.5 8.3 %copy-start.5 = (f32[128,6]{0,1:T(8,128)S(1)}, f32[128,6]{0,1:T(8,128)}, u32[]{:S(2)}) copy-start(f32[128,6]{0,1:T(8,128)} %param.29) | copy-start | bytes 9220
  121.5 157.8 %all-to-all-start.1 = ((bf16[32,2,16,2560]{3,2,1,0:T(8,128)(2,1)}), bf16[32,2,16,2560]{3,2,1,0:T(8,128)(2,1)}, u32[]{:S(2)}, u32[]{:S(2)}) async-start(bf16[32,2,16,2560]{3,2,1,0:T(8,128)(2,1)} %copy.66), calls=%async_computation.1 | async-start | bytes 10485760 | tf_op jit(solution)/shard_map/all_to_all | solution.py:105
  126.6 140.7 %all-reduce.3.cloned.1.call-start = ((), (), s32[]{:S(2)}) async-start(), calls=%async_computation.4 | async-start | bytes 1441792 | tf_op jit(solution)/shard_map/psum | solution.py:56
  129.1 178.2 %reduce-scatter.4.cloned.1.call-start = ((), (), s32[]{:S(2)}) async-start(), calls=%async_computation.3 | async-start | bytes 819200
  129.7 3.8 %copy-start.9 = (bf16[2560,768]{1,0:T(8,128)(2,1)S(1)}, bf16[2560,768]{1,0:T(8,128)(2,1)}, u32[]{:S(2)}) copy-start(bf16[2560,768]{1,0:T(8,128)(2,1)} %param.18) | copy-start | bytes 11796484
  133.5 2.1 copy-start.2
  282.7 3.5 %copy-start.3 = (bf16[16,16,640]{2,0,1:T(8,128)(2,1)S(1)}, bf16[16,16,640]{2,0,1:T(8,128)(2,1)}, u32[]{:S(2)}) copy-start(bf16[16,16,640]{2,0,1:T(8,128)(2,1)} %get-tuple-element.5) | copy-start | bytes 983044
Sparse Core Ops, SparseCore 0:
  130.8 136.4 all-reduce.2
  287.9 19.4 reduce-scatter.3
where the time goes:
time: 316 us
  waiting for transfers between devices  151 us (48%)
  blocking collectives  95.2 us (30%)
  matrix products  31.9 us (10%)
  local copies, waits for them, and re-layouts  14.3 us (5%)
  between operations  13.7 us (4%)
  starting transfers between devices  5.27 us (2%)
  other arithmetic  4.99 us (2%)
    psum x1, waiting for transfers between devices, body(): picked_in, picked_out = lax.psum((picked_in, picked_out), 'dp')  131 us
    all_to_all x1, blocking collectives, body(): lax.all_to_all(send_rows, 'dp', split_axis=0, concat_axis=0, tiled=True)  69.5 us
    unnamed x3, waiting for transfers between devices  19.6 us
    all_gather x1, blocking collectives, body(): gathered = lax.all_gather(hidden, 'mp', axis=1, tiled=True)  14.9 us
    dot_general x1, matrix products, experts_apply(): jnp.einsum('sjcf,jfd->sjcd', inner, expert_down, preferred_element_type=j...  12.8 us
    psum x1, blocking collectives, body(): lowrank_sel = lax.psum(lowrank_sel, 'mp')  10.8 us
    unnamed x25, local copies, waits for them, and re-layouts  7.3 us
  transfers between devices with their start and end apart: 3, of which 2 were waited for; matrix products, arithmetic and copies ran while one was open for 3% of the time, Pallas kernels for 0%

commit v1 on v0

--- a/solution.py
+++ b/solution.py
@@ -2,6 +2,14 @@
 import jax.numpy as jnp
 from jax import lax
 from jax.sharding import PartitionSpec as P
+
+
+def sum_by_hops(x, mesh_axis):
+    peers, total = (lax.axis_size(mesh_axis), x)
+    for far in [1 << k for k in range(peers.bit_length() - 1)]:
+        swap = [(i, i ^ far) for i in range(peers)]
+        total = total + lax.ppermute(total, mesh_axis, swap)
+    return total
 
 
 def experts_apply(slots_in, expert_gate, expert_up, expert_down):
@@ -79,7 +87,7 @@
     lowrank_sel = jnp.sum(
         lowrank.reshape(tok_rows, active_count, rank_width) * chosen[:, :, None], axis=1
     )
-    lowrank_sel = lax.psum(lowrank_sel, "mp")
+    lowrank_sel = sum_by_hops(lowrank_sel, "mp")
     lowrank = (chosen[:, :, None] * lowrank_sel[:, None, :]).reshape(
         tok_rows, active_count * rank_width
     )

time: 316 us -> 319 us (level)
  blocking collectives: 95.2 us -> 84.4 us
  waiting for transfers between devices: 151 us -> 157 us
  starting transfers between devices: 5.27 us -> 9.84 us
  matrix products: 31.9 us -> 35.4 us
    psum x1 -> x0, blocking collectives: 10.8 us -> none  [body(): lowrank_sel = lax.psum(lowrank_sel, 'mp')]
    ppermute x0 -> x2, starting transfers between devices: none -> 4.75 us  [sum_by_hops(): total = total + lax.ppermute(total, mesh_axis, swap)]
    unnamed x25 -> x23, local copies, waits for them, and re-layouts: 7.3 us -> 6.06 us
  transfers between devices with their start and end apart: 3 -> 5, of which waited for: 2 -> 3; matrix products, arithmetic and copies ran while one was open for 3% -> 4% of each run, Pallas kernels for 0% -> 0%
where the time goes in v1:
time: 319 us
  waiting for transfers between devices  157 us (49%)
  blocking collectives  84.4 us (26%)
  matrix products  35.4 us (11%)
  between operations  13.7 us (4%)
  local copies, waits for them, and re-layouts  13 us (4%)
  starting transfers between devices  9.84 us (3%)
  other arithmetic  4.99 us (2%)
    psum x1, waiting for transfers between devices, body(): picked_in, picked_out = lax.psum((picked_in, picked_out), 'dp')  134 us
    all_to_all x1, blocking collectives, body(): lax.all_to_all(send_rows, 'dp', split_axis=0, concat_axis=0, tiled=True)  69.5 us
    unnamed x3, waiting for transfers between devices  21.6 us
    all_gather x1, blocking collectives, body(): gathered = lax.all_gather(hidden, 'mp', axis=1, tiled=True)  14.9 us
    dot_general x1, matrix products, experts_apply(): jnp.einsum('sjcf,jfd->sjcd', inner, expert_down, preferred_element_type=j...  13.2 us
  transfers between devices with their start and end apart: 5, of which 3 were waited for; matrix products, arithmetic and copies ran while one was open for 4% of the time, Pallas kernels for 0%

profile of v1, /device:TPU:0, one launch (start us, length us, event | category | flops | bytes accessed | tf_op | source)
XLA Modules:
  0.0 318.6 jit_solution(10573686482799431132)
XLA Ops:
  6.5 0.8 copy.60
  7.7 1.8 reduce-window.18
  11.3 14.9 %all_gather.3 = bf16[128,2560]{1,0:T(8,128)(2,1)S(1)} all-gather(bf16[128,640]{1,0:T(8,128)(2,1)} %param.15), channel_id=1, replica_groups=mesh['dp'=32,'mp'=4] {'mp'}, dimensions={1}, use_global_device_ids=true | all-gather | bytes 819200 | tf_op jit(solution)/shard_map/all_gather | solution.py:65
  27.2 1.6 convolution_convert_fusion.1
  28.8 69.5 %all_to_all.10 = bf16[32,2,16,2560]{3,2,1,0:T(8,128)(2,1)S(1)} all-to-all(bf16[32,2,16,2560]{3,2,1,0:T(8,128)(2,1)S(1)} %bitcast.98), channel_id=1, replica_groups=mesh['dp'=32,'mp'=4] {'dp'}, dimensions={0} | all-to-all | bytes 10485760 | tf_op jit(solution)/shard_map/all_to_all | solution.py:115
  98.3 2.3 copy-done.1
  100.6 4.0 %fusion.3 = f32[2,32,16,384]{3,2,1,0:T(8,128)} fusion(bf16[32,2,16,2560]{3,2,1,0:T(8,128)(2,1)S(1)} %all_to_all.10, bf16[2,2560,384]{2,1,0:T(8,128)(2,1)S(1)} %copy-done.7), kind=kOutput, calls=%fused_computation.5 | convolution fusion | flops 2013265920 | bytes 10747904 | tf_op jit(solution)/shard_map/sjcd,jdf->sjcf/dot_general | solution.py:16
  104.6 13.2 %fusion = bf16[32,2,16,2560]{3,2,0,1:T(8,128)(2,1)} fusion(bf16[2,384,2560]{2,1,0:T(8,128)(2,1)} %param.22, f32[2,32,16,384]{3,2,1,0:T(8,128)} %fusion.3, bf16[2,2560,384]{2,1,0:T(8,128)(2,1)} %param.21, bf16[32,2,16,2560]{3,2,1,0:T(8,128)(2,1)} %copy-done.1), kind=kOutput, calls=%fused_computation.2 | convolution fusion | flops 4031512576 | bytes 19922944 | tf_op jit(solution)/shard_map/sjcf,jfd->sjcd/dot_general | solution.py:21
  117.8 5.3 %copy.66 = bf16[32,2,16,2560]{3,2,1,0:T(8,128)(2,1)} copy(bf16[32,2,16,2560]{3,2,0,1:T(8,128)(2,1)} %fusion) | data formatting | bytes 10485760 | tf_op jit(solution)/shard_map/convert_element_type | solution.py:119
  123.1 5.0 %all-to-all-start.1 = ((bf16[32,2,16,2560]{3,2,1,0:T(8,128)(2,1)}), bf16[32,2,16,2560]{3,2,1,0:T(8,128)(2,1)}, u32[]{:S(2)}, u32[]{:S(2)}) async-start(bf16[32,2,16,2560]{3,2,1,0:T(8,128)(2,1)} %copy.66), calls=%async_computation.1 | async-start | bytes 10485760 | tf_op jit(solution)/shard_map/all_to_all | solution.py:113
  128.7 0.9 copy.95
  129.5 1.1 convolution_convert_fusion.3
  131.3 3.0 fusion.57
  135.2 133.7 %all-reduce.3.cloned.1.call-done = (bf16[16,16,640]{2,0,1:T(8,128)(2,1)}, bf16[16,16,768]{2,1,0:T(8,128)(2,1)}) async-done(((bf16[16,16,640]{2,0,1:T(8,128)(2,1)}, bf16[16,16,768]{2,1,0:T(8,128)(2,1)}), (bf16[16,16,640]{2,0,1:T(8,128)(2,1)}, bf16[16,16,768]{2,1,0:T(8,128)(2,1)})) %all-reduce.3.cloned.1.call-update) | async-done | bytes 720912 | tf_op jit(solution)/shard_map/psum | solution.py:64
  268.9 1.3 fusion.29
  270.1 1.8 collective-permute-start
  271.9 2.8 fusion.59
  274.8 2.9 collective-permute-start.1
  278.1 1.9 collective-permute-done.1
  280.0 3.3 %fusion.39 = f32[128,2560]{1,0:T(8,128)S(1)} fusion(bf16[1024,2560]{1,0:T(8,128)(2,1)} %bitcast.11, f32[128,1024]{1,0:T(8,128)S(1)} %select_reduce_fusion), kind=kOutput, calls=%fused_computation.53 | convolution fusion | flops 671219712 | bytes 7077888 | tf_op jit(solution)/shard_map/dot_general | solution.py:129
  283.4 3.5 %fusion.8 = f32[128,2560]{1,0:T(8,128)S(1)} fusion(f32[128,2560]{1,0:T(8,128)S(1)} %fusion.59, f32[128,2560]{1,0:T(8,128)S(1)} %fusion.39, bf16[1024,2560]{1,0:T(8,128)(2,1)} %bitcast.11, f32[128,1024]{1,0:T(8,128)S(1)} %select_reduce_fusion), kind=kOutput, calls=%fused_computation.11 | convolution fusion | flops 672268288 | bytes 9699328 | tf_op jit(solution)/shard_map/dot_general | solution.py:129
  287.3 1.1 copy.75
  288.4 21.6 %reduce-scatter.4.cloned.1.call-done = bf16[640,128]{1,0:T(8,128)(2,1)} async-done(((bf16[2560,128]{1,0:T(8,128)(2,1)}), bf16[640,128]{1,0:T(8,128)(2,1)}) %reduce-scatter.4.cloned.1.call-update) | async-done | bytes 163856
  310.0 1.7 copy.76
  (54 shorter events, 5.8 us)
Async XLA Ops:
  6.5 123.0 %copy-start = (bf16[2,16,2560]{2,1,0:T(8,128)(2,1)S(1)}, bf16[2,16,2560]{2,1,0:T(8,128)(2,1)}, u32[]{:S(2)}) copy-start(bf16[2,16,2560]{2,1,0:T(8,128)(2,1)} %param.24) | copy-start | bytes 491524
  28.8 71.8 %copy-start.7 = (bf16[2,2560,384]{2,1,0:T(8,128)(2,1)S(1)}, bf16[2,2560,384]{2,1,0:T(8,128)(2,1)}, u32[]{:S(2)}) copy-start(bf16[2,2560,384]{2,1,0:T(8,128)(2,1)} %param.20) | copy-start | bytes 11796484
  98.3 2.3 copy-start.1
  123.1 5.1 %copy-start.3 = (bf16[2,768,16]{1,2,0:T(8,128)(2,1)S(1)}, bf16[2,768,16]{1,2,0:T(8,128)(2,1)}, u32[]{:S(2)}) copy-start(bf16[2,768,16]{1,2,0:T(8,128)(2,1)} %param.23) | copy-start | bytes 147460
  123.1 5.1 %copy-start.5 = (s32[16]{0:T(128)S(1)}, s32[16]{0:T(128)}, u32[]{:S(2)}) copy-start(s32[16]{0:T(128)} %param.25) | copy-start | bytes 196
  123.1 7.6 %copy-start.6 = (s32[64]{0:T(128)S(1)}, s32[64]{0:T(128)}, u32[]{:S(2)}) copy-start(s32[64]{0:T(128)} %param.26) | copy-start | bytes 772
  123.1 8.1 %copy-start.9 = (s32[64]{0:T(128)S(1)}, s32[64]{0:T(128)}, u32[]{:S(2)}) copy-start(s32[64]{0:T(128)} %param.27) | copy-start | bytes 772
  123.1 156.9 %all-to-all-start.1 = ((bf16[32,2,16,2560]{3,2,1,0:T(8,128)(2,1)}), bf16[32,2,16,2560]{3,2,1,0:T(8,128)(2,1)}, u32[]{:S(2)}, u32[]{:S(2)}) async-start(bf16[32,2,16,2560]{3,2,1,0:T(8,128)(2,1)} %copy.66), calls=%async_computation.1 | async-start | bytes 10485760 | tf_op jit(solution)/shard_map/all_to_all | solution.py:113
  128.1 140.7 %all-reduce.3.cloned.1.call-start = ((), (), s32[]{:S(2)}) async-start(), calls=%async_computation.4 | async-start | bytes 1441792 | tf_op jit(solution)/shard_map/psum | solution.py:64
  130.7 179.4 %reduce-scatter.4.cloned.1.call-start = ((), (), s32[]{:S(2)}) async-start(), calls=%async_computation.3 | async-start | bytes 819200
  131.1 3.3 %copy-start.8 = (bf16[2560,768]{1,0:T(8,128)(2,1)S(1)}, bf16[2560,768]{1,0:T(8,128)(2,1)}, u32[]{:S(2)}) copy-start(bf16[2560,768]{1,0:T(8,128)(2,1)} %param.18) | copy-start | bytes 11796484
  135.1 142.6 %copy-start.4 = (f32[128,6]{0,1:T(8,128)S(1)}, f32[128,6]{0,1:T(8,128)}, u32[]{:S(2)}) copy-start(f32[128,6]{0,1:T(8,128)} %param.29) | copy-start | bytes 9220
  270.1 4.6 %collective-permute-start = (f32[128,16]{0,1:T(8,128)S(1)}, f32[128,16]{0,1:T(8,128)S(1)}, u32[]{:S(2)}, u32[]{:S(2)}) collective-permute-start(f32[128,16]{0,1:T(8,128)S(1)} %fusion.29), channel_id=1, source_target_pairs={{0,1},{1,0},{2,3},{3,2},{4,5},{5,4},{6,7},{7,6},{8,9},{9,8},{10,11... | collective-permute-start | bytes 24584 | tf_op jit(solution)/shard_map/ppermute | solution.py:11
  274.8 5.2 %collective-permute-start.1 = (f32[128,16]{0,1:T(8,128)S(1)}, f32[128,16]{0,1:T(8,128)S(1)}, u32[]{:S(2)}, u32[]{:S(2)}) collective-permute-start(f32[128,16]{0,1:T(8,128)S(1)} %add.82), channel_id=1, source_target_pairs={{0,2},{1,3},{2,0},{3,1},{4,6},{5,7},{6,4},{7,5},{8,10},{9,11},{10,... | collective-permute-start | bytes 24584 | tf_op jit(solution)/shard_map/ppermute | solution.py:11
  283.4 3.5 %copy-start.2 = (bf16[16,16,640]{2,0,1:T(8,128)(2,1)S(1)}, bf16[16,16,640]{2,0,1:T(8,128)(2,1)}, u32[]{:S(2)}) copy-start(bf16[16,16,640]{2,0,1:T(8,128)(2,1)} %get-tuple-element.5) | copy-start | bytes 983044
Sparse Core Ops, SparseCore 0:
  132.3 136.4 all-reduce.2
  288.6 21.4 reduce-scatter.3
